TPU v7x, 128 devices: a whole 4x4x4 slice. The times are simulated.
128 devices in a mesh: grid: 32 (over y, x, core), layer: 4 (over z).
Axes of the slice: x: 4, y: 4, z: 4, core: 2. Of those that a mesh axis runs over, the one named last changes fastest.
Arguments:
- h_blocks: bfloat16 [1024, 8, 128, 128], P('grid', 'layer'), may hold values from -0.09375 to 0.09375
- block_cols: int32 [1024, 8], P('grid', 'layer'), may hold values from 0 to 1023, as said below
- t_now: bfloat16 [131072, 1536], P(('grid', 'layer')), may hold values from -6 to 6
- t_prev: bfloat16 [131072, 1536], P(('grid', 'layer')), may hold values from -6 to 6
Outputs:
- next_term: bfloat16 [131072, 1536], P(('grid', 'layer'))
- after_term: bfloat16 [131072, 1536], P(('grid', 'layer'))
Inputs may be any that keep to these rules, and one draw needn't show every extreme that they name: block_cols[i, 0] = i. With g = i // 32, every block column lies among the block rows g * 32 - 2 to g * 32 + 33 counted cyclically modulo 1024, and both ends of that range are named in every block row.
All inputs are finite; a program needn't handle non-finite values.
Results may differ from a plain program's by a relative error of at most 0.019.
Values may be sent and summed in bfloat16 or wider, within the bound.
No kernel may reach another device: no remote copies, remote signals or barrier semaphores. Data moves between devices by JAX's collectives and lax.ppermute only.
A program may use at most 192 MiB of HBM per device.

v0:
```python
import jax
import jax.numpy as jnp
from jax import lax
from jax.sharding import PartitionSpec as P

KB = 8
HB = 2
NCH = 4


def padded(array, width):
    size, length = (lax.axis_size("grid"), array.shape[0])
    up = [(i, (i + 1) % size) for i in range(size)]
    down = [(j, i) for i, j in up]
    before = lax.ppermute(array[length - width :], "grid", up)
    after = lax.ppermute(array[:width], "grid", down)
    return jnp.concatenate([before, array, after], axis=0)


def own_rows(h_own, rel_own, chunk):
    block_size = h_own.shape[2]
    panel = lax.all_gather(chunk, "layer", axis=0, tiled=True)
    wide = padded(panel, HB * block_size)
    blocks = wide.reshape(wide.shape[0] // block_size, block_size, chunk.shape[1])
    picked = blocks[rel_own]
    acc = jnp.einsum("rsij,rsjc->ric", h_own, picked, preferred_element_type=jnp.float32)
    return acc.reshape(chunk.shape[0], chunk.shape[1])


def shards(h_blocks, block_cols, t_now, t_prev):
    group_rows = h_blocks.shape[0]
    total_blocks = group_rows * lax.axis_size("grid")
    first_block = lax.axis_index("grid") * group_rows
    relative = (block_cols - first_block + HB + total_blocks) % total_blocks
    h_own = lax.all_to_all(h_blocks, "layer", 0, 1, tiled=True)
    rel_own = lax.all_to_all(relative, "layer", 0, 1, tiled=True)
    width = t_now.shape[1]
    step = width // NCH

    def recur(current, previous):
        outs = []
        for c in range(NCH):
            acc = own_rows(h_own, rel_own, current[c])
            outs.append((2.0 * acc - previous[c].astype(jnp.float32)).astype(jnp.bfloat16))
        return outs

    now_chunks = [t_now[:, c * step : (c + 1) * step] for c in range(NCH)]
    prev_chunks = [t_prev[:, c * step : (c + 1) * step] for c in range(NCH)]
    next_chunks = recur(now_chunks, prev_chunks)
    after_chunks = recur(next_chunks, now_chunks)
    return (jnp.concatenate(next_chunks, axis=1), jnp.concatenate(after_chunks, axis=1))


def solution(mesh):
    in_specs = (
        P("grid", "layer", None, None),
        P("grid", "layer"),
        P(("grid", "layer"), None),
        P(("grid", "layer"), None),
    )
    out_specs = (P(("grid", "layer"), None), P(("grid", "layer"), None))
    return jax.shard_map(shards, mesh=mesh, in_specs=in_specs, out_specs=out_specs, check_vma=False)
```

profile of v0, /device:TPU:0, one launch (start us, length us, event | category | flops | bytes accessed | tf_op | source)
XLA Modules:
  0.0 535.9 jit_solution(12677658248927611347)
XLA Ops:
  13.1 10.5 %all_to_all.37 = s32[4,8,2]{1,2,0:T(2,128)S(1)} all-to-all(s32[4,8,2]{1,2,0:T(2,128)S(1)} %copy.9), channel_id=1, replica_groups=mesh['grid'=32,'layer'=4] {'layer'}, dimensions={0} | all-to-all | bytes 512 | tf_op jit(solution)/shard_map/all_to_all | solution.py:36
  27.4 48.1 %all-to-all-done.1 = bf16[32,2,128,128]{3,2,1,0:T(8,128)(2,1)S(1)} async-done(((bf16[32,2,128,128]{3,2,1,0:T(8,128)(2,1)}), bf16[32,2,128,128]{3,2,1,0:T(8,128)(2,1)S(1)}, u32[]{:S(2)}, u32[]{:S(2)}) %all-to-all-start.1) | async-done | bytes 2097184 | tf_op jit(solution)/shard_map/all_to_all | solution.py:35
  84.8 32.1 %all-gather.13.cloned.1.call-done = bf16[4096,384]{1,0:T(8,128)(2,1)} async-done(((bf16[1024,384]{1,0:T(8,128)(2,1)}), bf16[4096,384]{1,0:T(8,128)(2,1)}) %all-gather.13.cloned.1.call-update) | async-done | bytes 3145744 | tf_op jit(solution)/shard_map/all_gather | solution.py:22
  118.8 5.1 collective-permute-start.5
  123.8 34.6 %all-gather.11.cloned.1.call-done = bf16[4096,384]{1,0:T(8,128)(2,1)} async-done(((bf16[1024,384]{1,0:T(8,128)(2,1)}), bf16[4096,384]{1,0:T(8,128)(2,1)}) %all-gather.11.cloned.1.call-update) | async-done | bytes 3145744 | tf_op jit(solution)/shard_map/all_gather | solution.py:22
  160.2 40.0 %all-gather.9.cloned.1.call-done = bf16[4096,384]{1,0:T(8,128)(2,1)} async-done(((bf16[1024,384]{1,0:T(8,128)(2,1)}), bf16[4096,384]{1,0:T(8,128)(2,1)}) %all-gather.9.cloned.1.call-update) | async-done | bytes 3145744 | tf_op jit(solution)/shard_map/all_gather | solution.py:22
  206.2 7.1 %pad_maximum_fusion.3 = bf16[4608,384]{1,0:T(8,128)(2,1)} fusion(bf16[256,384]{1,0:T(8,128)(2,1)S(1)} %collective-permute-done.7, bf16[4096,384]{1,0:T(8,128)(2,1)} %all-gather.15.cloned.1.call-done, bf16[256,384]{1,0:T(8,128)(2,1)S(1)} %collective-permute-done.6), kind=kLoop, calls=%fused_computation.11 | loop fusion | flops 10616832 | bytes 7077888 | tf_op jit(solution)/shard_map/concatenate | solution.py:17
  213.3 6.1 %gather_fusion.3 = bf16[64,128,384]{2,1,0:T(8,128)(2,1)} fusion(bf16[36,128,384]{2,1,0:T(8,128)(2,1)} %bitcast.132, s32[1024]{0:T(1024)S(1)} %pad_clamp_fusion), kind=kCustom, calls=%fused_computation.3 | custom fusion | bytes 12583168 | tf_op jit(solution)/shard_map/gather | solution.py:25
  219.4 5.6 %collective-permute-start.1 = (bf16[256,384]{1,0:T(8,128)(2,1)S(1)}, bf16[256,384]{1,0:T(8,128)(2,1)S(1)}, u32[]{:S(2)}, u32[]{:S(2)}) collective-permute-start(bf16[256,384]{1,0:T(8,128)(2,1)S(1)} %copy-done.16), channel_id=1, source_target_pairs={{4,0},{8,4},{12,8},{16,12},{20,16},{24,20},{28,24},{32,28},{36,32}... | collective-permute-start | bytes 589832 | tf_op jit(solution)/shard_map/ppermute | solution.py:16
  224.9 7.0 %pad_maximum_fusion.2 = bf16[4608,384]{1,0:T(8,128)(2,1)} fusion(bf16[256,384]{1,0:T(8,128)(2,1)S(1)} %collective-permute-done.5, bf16[4096,384]{1,0:T(8,128)(2,1)} %all-gather.13.cloned.1.call-done, bf16[256,384]{1,0:T(8,128)(2,1)S(1)} %collective-permute-done.4), kind=kLoop, calls=%fused_computation.10 | loop fusion | flops 10616832 | bytes 7077888 | tf_op jit(solution)/shard_map/concatenate | solution.py:17
  232.0 6.1 %gather_fusion.2 = bf16[64,128,384]{2,1,0:T(8,128)(2,1)} fusion(bf16[36,128,384]{2,1,0:T(8,128)(2,1)} %bitcast.133, s32[1024]{0:T(1024)S(1)} %pad_clamp_fusion), kind=kCustom, calls=%fused_computation.2 | custom fusion | bytes 12583168 | tf_op jit(solution)/shard_map/gather | solution.py:25
  238.1 5.3 bitcast_multiply_fusion.4
  245.9 6.3 %pad_maximum_fusion.1 = bf16[4608,384]{1,0:T(8,128)(2,1)} fusion(bf16[256,384]{1,0:T(8,128)(2,1)S(1)} %collective-permute-done.3, bf16[4096,384]{1,0:T(8,128)(2,1)S(1)} %copy-done.11, bf16[256,384]{1,0:T(8,128)(2,1)S(1)} %collective-permute-done.2), kind=kLoop, calls=%fused_computation.9 | loop fusion | flops 10616832 | bytes 7077888 | tf_op jit(solution)/shard_map/concatenate | solution.py:17
  252.2 6.1 %gather_fusion.1 = bf16[64,128,384]{2,1,0:T(8,128)(2,1)} fusion(bf16[36,128,384]{2,1,0:T(8,128)(2,1)} %bitcast.134, s32[1024]{0:T(1024)S(1)} %pad_clamp_fusion), kind=kCustom, calls=%fused_computation.1 | custom fusion | bytes 12583168 | tf_op jit(solution)/shard_map/gather | solution.py:25
  258.3 5.3 bitcast_multiply_fusion.6
  263.6 6.5 %pad_maximum_fusion = bf16[4608,384]{1,0:T(8,128)(2,1)} fusion(bf16[256,384]{1,0:T(8,128)(2,1)S(1)} %collective-permute-done.1, bf16[4096,384]{1,0:T(8,128)(2,1)S(1)} %copy-done.10, bf16[256,384]{1,0:T(8,128)(2,1)S(1)} %collective-permute-done), kind=kLoop, calls=%fused_computation.8 | loop fusion | flops 10616832 | bytes 7077888 | tf_op jit(solution)/shard_map/concatenate | solution.py:17
  270.1 6.1 %gather_fusion = bf16[64,128,384]{2,1,0:T(8,128)(2,1)} fusion(bf16[36,128,384]{2,1,0:T(8,128)(2,1)} %bitcast.135, s32[1024]{0:T(1024)S(1)} %pad_clamp_fusion), kind=kCustom, calls=%fused_computation | custom fusion | bytes 12583168 | tf_op jit(solution)/shard_map/gather | solution.py:25
  288.6 29.9 %all-gather.23.cloned.1.call-done = bf16[4096,384]{1,0:T(8,128)(2,1)} async-done(((bf16[1024,384]{1,0:T(8,128)(2,1)}), bf16[4096,384]{1,0:T(8,128)(2,1)}) %all-gather.23.cloned.1.call-update) | async-done | bytes 3145744 | tf_op jit(solution)/shard_map/all_gather | solution.py:22
  324.7 35.1 %all-gather.21.cloned.1.call-done = bf16[4096,384]{1,0:T(8,128)(2,1)} async-done(((bf16[1024,384]{1,0:T(8,128)(2,1)}), bf16[4096,384]{1,0:T(8,128)(2,1)}) %all-gather.21.cloned.1.call-update) | async-done | bytes 3145744 | tf_op jit(solution)/shard_map/all_gather | solution.py:22
  366.7 34.6 %all-gather.19.cloned.1.call-done = bf16[4096,384]{1,0:T(8,128)(2,1)} async-done(((bf16[1024,384]{1,0:T(8,128)(2,1)}), bf16[4096,384]{1,0:T(8,128)(2,1)}) %all-gather.19.cloned.1.call-update) | async-done | bytes 3145744 | tf_op jit(solution)/shard_map/all_gather | solution.py:22
  403.1 40.2 %all-gather.17.cloned.1.call-done = bf16[4096,384]{1,0:T(8,128)(2,1)} async-done(((bf16[1024,384]{1,0:T(8,128)(2,1)}), bf16[4096,384]{1,0:T(8,128)(2,1)}) %all-gather.17.cloned.1.call-update) | async-done | bytes 3145744 | tf_op jit(solution)/shard_map/all_gather | solution.py:22
  449.2 7.1 %pad_maximum_fusion.7 = bf16[4608,384]{1,0:T(8,128)(2,1)} fusion(bf16[256,384]{1,0:T(8,128)(2,1)S(1)} %collective-permute-done.15, bf16[4096,384]{1,0:T(8,128)(2,1)} %all-gather.23.cloned.1.call-done, bf16[256,384]{1,0:T(8,128)(2,1)S(1)} %collective-permute-done.14), kind=kLoop, calls=%fused_computation.15 | loop fusion | flops 10616832 | bytes 7077888 | tf_op jit(solution)/shard_map/concatenate | solution.py:17
  456.3 6.1 %gather_fusion.7 = bf16[64,128,384]{2,1,0:T(8,128)(2,1)} fusion(bf16[36,128,384]{2,1,0:T(8,128)(2,1)} %bitcast.136, s32[1024]{0:T(1024)S(1)} %pad_clamp_fusion), kind=kCustom, calls=%fused_computation.7 | custom fusion | bytes 12583168 | tf_op jit(solution)/shard_map/gather | solution.py:25
  462.3 5.4 %bitcast_multiply_fusion = f32[8,384,128]{1,2,0:T(8,128)} fusion(bf16[8,8,128,128]{3,2,1,0:T(8,128)(2,1)S(1)} %bitcast.119, bf16[8,8,128,384]{3,2,1,0:T(8,128)(2,1)} %bitcast.128), kind=kOutput, calls=%fused_computation.34 | convolution fusion | flops 805699584 | bytes 9961472 | tf_op jit(solution)/shard_map/rsij,rsjc->ric/dot_general | solution.py:26
  472.8 6.5 %pad_maximum_fusion.6 = bf16[4608,384]{1,0:T(8,128)(2,1)} fusion(bf16[256,384]{1,0:T(8,128)(2,1)S(1)} %collective-permute-done.13, bf16[4096,384]{1,0:T(8,128)(2,1)S(1)} %copy-done.14, bf16[256,384]{1,0:T(8,128)(2,1)S(1)} %collective-permute-done.12), kind=kLoop, calls=%fused_computation.14 | loop fusion | flops 10616832 | bytes 7077888 | tf_op jit(solution)/shard_map/concatenate | solution.py:17
  479.2 6.1 %gather_fusion.6 = bf16[64,128,384]{2,1,0:T(8,128)(2,1)} fusion(bf16[36,128,384]{2,1,0:T(8,128)(2,1)} %bitcast.137, s32[1024]{0:T(1024)S(1)} %pad_clamp_fusion), kind=kCustom, calls=%fused_computation.6 | custom fusion | bytes 12583168 | tf_op jit(solution)/shard_map/gather | solution.py:25
  485.3 5.4 %bitcast_multiply_fusion.1 = f32[8,384,128]{1,2,0:T(8,128)} fusion(bf16[8,8,128,128]{3,2,1,0:T(8,128)(2,1)S(1)} %bitcast.120, bf16[8,8,128,384]{3,2,1,0:T(8,128)(2,1)} %bitcast.129), kind=kOutput, calls=%fused_computation.35 | convolution fusion | flops 805699584 | bytes 9961472 | tf_op jit(solution)/shard_map/rsij,rsjc->ric/dot_general | solution.py:26
  490.7 6.3 %pad_maximum_fusion.5 = bf16[4608,384]{1,0:T(8,128)(2,1)} fusion(bf16[256,384]{1,0:T(8,128)(2,1)S(1)} %collective-permute-done.11, bf16[4096,384]{1,0:T(8,128)(2,1)S(1)} %copy-done.13, bf16[256,384]{1,0:T(8,128)(2,1)S(1)} %collective-permute-done.10), kind=kLoop, calls=%fused_computation.13 | loop fusion | flops 10616832 | bytes 7077888 | tf_op jit(solution)/shard_map/concatenate | solution.py:17
  497.0 6.1 %gather_fusion.5 = bf16[64,128,384]{2,1,0:T(8,128)(2,1)} fusion(bf16[36,128,384]{2,1,0:T(8,128)(2,1)} %bitcast.138, s32[1024]{0:T(1024)S(1)} %pad_clamp_fusion), kind=kCustom, calls=%fused_computation.5 | custom fusion | bytes 12583168 | tf_op jit(solution)/shard_map/gather | solution.py:25
  503.0 5.3 bitcast_multiply_fusion.2
  508.4 6.5 %pad_maximum_fusion.4 = bf16[4608,384]{1,0:T(8,128)(2,1)} fusion(bf16[256,384]{1,0:T(8,128)(2,1)S(1)} %collective-permute-done.9, bf16[4096,384]{1,0:T(8,128)(2,1)S(1)} %copy-done.12, bf16[256,384]{1,0:T(8,128)(2,1)S(1)} %collective-permute-done.8), kind=kLoop, calls=%fused_computation.12 | loop fusion | flops 10616832 | bytes 7077888 | tf_op jit(solution)/shard_map/concatenate | solution.py:17
  514.9 6.1 %gather_fusion.4 = bf16[64,128,384]{2,1,0:T(8,128)(2,1)} fusion(bf16[36,128,384]{2,1,0:T(8,128)(2,1)} %bitcast.131, s32[1024]{0:T(1024)S(1)} %pad_clamp_fusion), kind=kCustom, calls=%fused_computation.4 | custom fusion | bytes 12583168 | tf_op jit(solution)/shard_map/gather | solution.py:25
  (110 shorter events, 76.9 us)
Async XLA Ops:
  7.2 5.8 %copy-start.18 = (s32[32,2]{0,1:T(2,128)S(1)}, s32[32,2]{0,1:T(2,128)}, u32[]{:S(2)}) copy-start(s32[32,2]{0,1:T(2,128)} %param.5) | copy-start | bytes 772
  7.2 71.4 %all-gather.15.cloned.1.call-start = ((), (), s32[]{:S(2)}) async-start(), calls=%async_computation.5 | async-start | bytes 3932160 | tf_op jit(solution)/shard_map/all_gather | solution.py:22
  10.9 106.1 %all-gather.13.cloned.1.call-start = ((), (), s32[]{:S(2)}) async-start(), calls=%async_computation.4 | async-start | bytes 3932160 | tf_op jit(solution)/shard_map/all_gather | solution.py:22
  11.6 146.8 %all-gather.11.cloned.1.call-start = ((), (), s32[]{:S(2)}) async-start(), calls=%async_computation.3 | async-start | bytes 3932160 | tf_op jit(solution)/shard_map/all_gather | solution.py:22
  12.4 187.9 %all-gather.9.cloned.1.call-start = ((), (), s32[]{:S(2)}) async-start(), calls=%async_computation.2 | async-start | bytes 3932160 | tf_op jit(solution)/shard_map/all_gather | solution.py:22
  23.6 52.0 %all-to-all-start.1 = ((bf16[32,2,128,128]{3,2,1,0:T(8,128)(2,1)}), bf16[32,2,128,128]{3,2,1,0:T(8,128)(2,1)S(1)}, u32[]{:S(2)}, u32[]{:S(2)}) async-start(bf16[32,2,128,128]{3,2,1,0:T(8,128)(2,1)} %param.4), calls=%async_computation.1 | async-start | bytes 4194304 | tf_op jit(solution)/shard_map/all_to_all | solution.py:35
  27.2 291.3 %all-gather.23.cloned.1.call-start = ((), (), s32[]{:S(2)}) async-start(), calls=%async_computation.9 | async-start | bytes 3932160 | tf_op jit(solution)/shard_map/all_gather | solution.py:22
  79.7 122.4 %collective-permute-start.6 = (bf16[256,384]{1,0:T(8,128)(2,1)S(1)}, bf16[256,384]{1,0:T(8,128)(2,1)S(1)}, u32[]{:S(2)}, u32[]{:S(2)}) collective-permute-start(bf16[256,384]{1,0:T(8,128)(2,1)S(1)} %get-tuple-element.28), channel_id=1, source_target_pairs={{0,4},{4,8},{8,12},{12,16},{16,20},{20,24},{24,28},{28,32},{32,36}... | collective-permute-start | bytes 589832 | tf_op jit(solution)/shard_map/ppermute | solution.py:15
  79.8 126.4 %collective-permute-start.7 = (bf16[256,384]{1,0:T(8,128)(2,1)S(1)}, bf16[256,384]{1,0:T(8,128)(2,1)S(1)}, u32[]{:S(2)}, u32[]{:S(2)}) collective-permute-start(bf16[256,384]{1,0:T(8,128)(2,1)S(1)} %get-tuple-element.29), channel_id=1, source_target_pairs={{4,0},{8,4},{12,8},{16,12},{20,16},{24,20},{28,24},{32,28},{36,32}... | collective-permute-start | bytes 589832 | tf_op jit(solution)/shard_map/ppermute | solution.py:16
  118.8 100.6 %collective-permute-start.4 = (bf16[256,384]{1,0:T(8,128)(2,1)}, bf16[256,384]{1,0:T(8,128)(2,1)S(1)}, u32[]{:S(2)}, u32[]{:S(2)}) collective-permute-start(bf16[256,384]{1,0:T(8,128)(2,1)} %get-tuple-element.26), channel_id=1, source_target_pairs={{0,4},{4,8},{8,12},{12,16},{16,20},{20,24},{24,28},{28,32},{32,36}... | collective-permute-start | bytes 589832 | tf_op jit(solution)/shard_map/ppermute | solution.py:15
  118.8 106.2 %collective-permute-start.5 = (bf16[256,384]{1,0:T(8,128)(2,1)}, bf16[256,384]{1,0:T(8,128)(2,1)S(1)}, u32[]{:S(2)}, u32[]{:S(2)}) collective-permute-start(bf16[256,384]{1,0:T(8,128)(2,1)} %get-tuple-element.27), channel_id=1, source_target_pairs={{4,0},{8,4},{12,8},{16,12},{20,16},{24,20},{28,24},{32,28},{36,32}... | collective-permute-start | bytes 589832 | tf_op jit(solution)/shard_map/ppermute | solution.py:16
  160.2 85.7 %collective-permute-start.2 = (bf16[256,384]{1,0:T(8,128)(2,1)}, bf16[256,384]{1,0:T(8,128)(2,1)S(1)}, u32[]{:S(2)}, u32[]{:S(2)}) collective-permute-start(bf16[256,384]{1,0:T(8,128)(2,1)} %get-tuple-element.24), channel_id=1, source_target_pairs={{0,4},{4,8},{8,12},{12,16},{16,20},{20,24},{24,28},{28,32},{32,36}... | collective-permute-start | bytes 589832 | tf_op jit(solution)/shard_map/ppermute | solution.py:15
  202.1 43.9 %collective-permute-start.3 = (bf16[256,384]{1,0:T(8,128)(2,1)}, bf16[256,384]{1,0:T(8,128)(2,1)S(1)}, u32[]{:S(2)}, u32[]{:S(2)}) collective-permute-start(bf16[256,384]{1,0:T(8,128)(2,1)} %get-tuple-element.25), channel_id=1, source_target_pairs={{4,0},{8,4},{12,8},{16,12},{20,16},{24,20},{28,24},{32,28},{36,32}... | collective-permute-start | bytes 589832 | tf_op jit(solution)/shard_map/ppermute | solution.py:16
  206.2 57.4 %collective-permute-start = (bf16[256,384]{1,0:T(8,128)(2,1)}, bf16[256,384]{1,0:T(8,128)(2,1)S(1)}, u32[]{:S(2)}, u32[]{:S(2)}) collective-permute-start(bf16[256,384]{1,0:T(8,128)(2,1)} %get-tuple-element.18), channel_id=1, source_target_pairs={{0,4},{4,8},{8,12},{12,16},{16,20},{20,24},{24,28},{28,32},{32,36}... | collective-permute-start | bytes 589832 | tf_op jit(solution)/shard_map/ppermute | solution.py:15
  213.3 6.1 %copy-start.16 = (bf16[256,384]{1,0:T(8,128)(2,1)S(1)}, bf16[256,384]{1,0:T(8,128)(2,1)}, u32[]{:S(2)}) copy-start(bf16[256,384]{1,0:T(8,128)(2,1)} %get-tuple-element.19) | copy-start | bytes 589828
  219.4 44.2 %collective-permute-start.1 = (bf16[256,384]{1,0:T(8,128)(2,1)S(1)}, bf16[256,384]{1,0:T(8,128)(2,1)S(1)}, u32[]{:S(2)}, u32[]{:S(2)}) collective-permute-start(bf16[256,384]{1,0:T(8,128)(2,1)S(1)} %copy-done.16), channel_id=1, source_target_pairs={{4,0},{8,4},{12,8},{16,12},{20,16},{24,20},{28,24},{32,28},{36,32}... | collective-permute-start | bytes 589832 | tf_op jit(solution)/shard_map/ppermute | solution.py:16
  258.3 5.4 copy-start.10
  283.5 76.3 %all-gather.21.cloned.1.call-start = ((), (), s32[]{:S(2)}) async-start(), calls=%async_computation.8 | async-start | bytes 3932160 | tf_op jit(solution)/shard_map/all_gather | solution.py:22
  284.1 117.2 %all-gather.19.cloned.1.call-start = ((), (), s32[]{:S(2)}) async-start(), calls=%async_computation.7 | async-start | bytes 3932160 | tf_op jit(solution)/shard_map/all_gather | solution.py:22
  284.8 158.4 %all-gather.17.cloned.1.call-start = ((), (), s32[]{:S(2)}) async-start(), calls=%async_computation.6 | async-start | bytes 3932160 | tf_op jit(solution)/shard_map/all_gather | solution.py:22
  319.6 125.5 %collective-permute-start.14 = (bf16[256,384]{1,0:T(8,128)(2,1)S(1)}, bf16[256,384]{1,0:T(8,128)(2,1)S(1)}, u32[]{:S(2)}, u32[]{:S(2)}) collective-permute-start(bf16[256,384]{1,0:T(8,128)(2,1)S(1)} %get-tuple-element.12), channel_id=1, source_target_pairs={{0,4},{4,8},{8,12},{12,16},{16,20},{20,24},{24,28},{28,32},{32,36}... | collective-permute-start | bytes 589832 | tf_op jit(solution)/shard_map/ppermute | solution.py:15
  319.7 129.5 %collective-permute-start.15 = (bf16[256,384]{1,0:T(8,128)(2,1)S(1)}, bf16[256,384]{1,0:T(8,128)(2,1)S(1)}, u32[]{:S(2)}, u32[]{:S(2)}) collective-permute-start(bf16[256,384]{1,0:T(8,128)(2,1)S(1)} %get-tuple-element.13), channel_id=1, source_target_pairs={{4,0},{8,4},{12,8},{16,12},{20,16},{24,20},{28,24},{32,28},{36,32}... | collective-permute-start | bytes 589832 | tf_op jit(solution)/shard_map/ppermute | solution.py:16
  361.6 106.1 %collective-permute-start.12 = (bf16[256,384]{1,0:T(8,128)(2,1)}, bf16[256,384]{1,0:T(8,128)(2,1)S(1)}, u32[]{:S(2)}, u32[]{:S(2)}) collective-permute-start(bf16[256,384]{1,0:T(8,128)(2,1)} %get-tuple-element.10), channel_id=1, source_target_pairs={{0,4},{4,8},{8,12},{12,16},{16,20},{20,24},{24,28},{28,32},{32,36}... | collective-permute-start | bytes 589832 | tf_op jit(solution)/shard_map/ppermute | solution.py:15
  361.6 111.1 %collective-permute-start.13 = (bf16[256,384]{1,0:T(8,128)(2,1)}, bf16[256,384]{1,0:T(8,128)(2,1)S(1)}, u32[]{:S(2)}, u32[]{:S(2)}) collective-permute-start(bf16[256,384]{1,0:T(8,128)(2,1)} %get-tuple-element.11), channel_id=1, source_target_pairs={{4,0},{8,4},{12,8},{16,12},{20,16},{24,20},{28,24},{32,28},{36,32}... | collective-permute-start | bytes 589832 | tf_op jit(solution)/shard_map/ppermute | solution.py:16
  403.1 87.6 %collective-permute-start.10 = (bf16[256,384]{1,0:T(8,128)(2,1)}, bf16[256,384]{1,0:T(8,128)(2,1)S(1)}, u32[]{:S(2)}, u32[]{:S(2)}) collective-permute-start(bf16[256,384]{1,0:T(8,128)(2,1)} %get-tuple-element.8), channel_id=1, source_target_pairs={{0,4},{4,8},{8,12},{12,16},{16,20},{20,24},{24,28},{28,32},{32,36}... | collective-permute-start | bytes 589832 | tf_op jit(solution)/shard_map/ppermute | solution.py:15
  445.0 45.6 %collective-permute-start.11 = (bf16[256,384]{1,0:T(8,128)(2,1)}, bf16[256,384]{1,0:T(8,128)(2,1)S(1)}, u32[]{:S(2)}, u32[]{:S(2)}) collective-permute-start(bf16[256,384]{1,0:T(8,128)(2,1)} %get-tuple-element.9), channel_id=1, source_target_pairs={{4,0},{8,4},{12,8},{16,12},{20,16},{24,20},{28,24},{32,28},{36,32}... | collective-permute-start | bytes 589832 | tf_op jit(solution)/shard_map/ppermute | solution.py:16
  449.2 59.2 %collective-permute-start.8 = (bf16[256,384]{1,0:T(8,128)(2,1)}, bf16[256,384]{1,0:T(8,128)(2,1)S(1)}, u32[]{:S(2)}, u32[]{:S(2)}) collective-permute-start(bf16[256,384]{1,0:T(8,128)(2,1)} %get-tuple-element.6), channel_id=1, source_target_pairs={{0,4},{4,8},{8,12},{12,16},{16,20},{20,24},{24,28},{28,32},{32,36}... | collective-permute-start | bytes 589832 | tf_op jit(solution)/shard_map/ppermute | solution.py:15
  462.3 5.4 %copy-start.17 = (bf16[256,384]{1,0:T(8,128)(2,1)S(1)}, bf16[256,384]{1,0:T(8,128)(2,1)}, u32[]{:S(2)}) copy-start(bf16[256,384]{1,0:T(8,128)(2,1)} %get-tuple-element.7) | copy-start | bytes 589828
  462.3 10.4 %copy-start.14 = (bf16[4096,384]{1,0:T(8,128)(2,1)S(1)}, bf16[4096,384]{1,0:T(8,128)(2,1)}, u32[]{:S(2)}) copy-start(bf16[4096,384]{1,0:T(8,128)(2,1)} %all-gather.21.cloned.1.call-done) | copy-start | bytes 9437188
  467.7 40.7 %collective-permute-start.9 = (bf16[256,384]{1,0:T(8,128)(2,1)S(1)}, bf16[256,384]{1,0:T(8,128)(2,1)S(1)}, u32[]{:S(2)}, u32[]{:S(2)}) collective-permute-start(bf16[256,384]{1,0:T(8,128)(2,1)S(1)} %copy-done.17), channel_id=1, source_target_pairs={{4,0},{8,4},{12,8},{16,12},{20,16},{24,20},{28,24},{32,28},{36,32}... | collective-permute-start | bytes 589832 | tf_op jit(solution)/shard_map/ppermute | solution.py:16
  485.3 5.4 %copy-start.13 = (bf16[4096,384]{1,0:T(8,128)(2,1)S(1)}, bf16[4096,384]{1,0:T(8,128)(2,1)}, u32[]{:S(2)}) copy-start(bf16[4096,384]{1,0:T(8,128)(2,1)} %all-gather.19.cloned.1.call-done) | copy-start | bytes 9437188
  503.0 5.4 copy-start.12
  (12 other events, 47.2 us)
Sparse Core Ops, SparseCore 0:
  11.0 64.1 all-gather.14
  76.8 40.1 all-gather.12
  118.6 39.7 all-gather.10
  160.5 39.7 all-gather.8
  283.6 34.8 all-gather.22
  320.0 39.7 all-gather.20
  361.5 39.7 all-gather.18
  403.5 39.7 all-gather.16
where the time goes:
time: 542 us; the launch traced here: 536 us
  waiting for transfers between devices  298 us (55%)
  local copies, waits for them, and re-layouts  70.3 us (13%)
  other arithmetic  61 us (11%)
  starting transfers between devices  43.2 us (8%)
  matrix products  37.6 us (7%)
  between operations  14.8 us (3%)
  blocking collectives  10.5 us (2%)
    all_gather x8, waiting for transfers between devices, own_rows(): panel = lax.all_gather(chunk, 'layer', axis=0, tiled=True)  246 us
    concatenate x8, other arithmetic, padded(): return jnp.concatenate([before, array, after], axis=0)  53.2 us
    gather x8, local copies, waits for them, and re-layouts, own_rows(): picked = blocks[rel_own]  48.5 us
    all_to_all x1, waiting for transfers between devices, shards(): h_own = lax.all_to_all(h_blocks, 'layer', 0, 1, tiled=True)  48.1 us
    ppermute x8, starting transfers between devices, padded(): after = lax.ppermute(array[:width], 'grid', down)  39.1 us
    dot_general x8, matrix products, own_rows(): jnp.einsum('rsij,rsjc->ric', h_own, picked, preferred_element_type=jnp.fl...  37.6 us
    slice x8, local copies, waits for them, and re-layouts, padded(): before = lax.ppermute(array[length - width:], 'grid', up)  13 us
  transfers between devices with their start and end apart: 25, of which 8 were waited for; matrix products, arithmetic and copies ran while one was open for 23% of the time, Pallas kernels for 0%

commit v1 on v0

--- a/solution.py
+++ b/solution.py
@@ -19,7 +19,9 @@
 
 def own_rows(h_own, rel_own, chunk):
     block_size = h_own.shape[2]
-    panel = lax.all_gather(chunk, "layer", axis=0, tiled=True)
+    panel = jnp.concatenate(
+        lax.all_to_all(jnp.stack([chunk] * lax.axis_size("layer")), "layer", 0, 0), axis=0
+    )
     wide = padded(panel, HB * block_size)
     blocks = wide.reshape(wide.shape[0] // block_size, block_size, chunk.shape[1])
     picked = blocks[rel_own]

time: 542 us -> 522 us (0.963)
  waiting for transfers between devices: 298 us -> 50.1 us
  blocking collectives: 10.5 us -> 235 us
  between operations: 14.8 us -> 1.08 us
  starting transfers between devices: 43.2 us -> 53 us
  local copies, waits for them, and re-layouts: 70.3 us -> 76 us
    all_gather x8 -> x0, waiting for transfers between devices: 246 us -> none  [own_rows(): panel = lax.all_gather(chunk, 'layer', axis=0, tiled=True)]
    all_to_all x0 -> x6, blocking collectives: none -> 224 us  [own_rows(): lax.all_to_all(jnp.stack([chunk] * lax.axis_size('layer')), 'layer', 0, 0)]
    all_to_all x0 -> x2, waiting for transfers between devices: none -> 28.2 us  [own_rows(): lax.all_to_all(jnp.stack([chunk] * lax.axis_size('layer')), 'layer', 0, 0)]
    all_to_all x1, waiting for transfers between devices: 48.1 us -> 21.8 us  [shards(): h_own = lax.all_to_all(h_blocks, 'layer', 0, 1, tiled=True)]
    all_to_all x0 -> x2, starting transfers between devices: none -> 9.32 us  [own_rows(): lax.all_to_all(jnp.stack([chunk] * lax.axis_size('layer')), 'layer', 0, 0)]
    another operation x0 -> x8, local copies, waits for them, and re-layouts: none -> 7.17 us  [own_rows(): jnp.stack([chunk] * lax.axis_size('layer'))]
  transfers between devices with their start and end apart: 25 -> 19, of which waited for: 8 -> 3; matrix products, arithmetic and copies ran while one was open for 23% -> 25% of each run, Pallas kernels for 0% -> 0%
where the time goes in v1:
time: 522 us; the launch traced here: 514 us
  blocking collectives  235 us (45%)
  local copies, waits for them, and re-layouts  76 us (15%)
  other arithmetic  62.2 us (12%)
  starting transfers between devices  53 us (10%)
  waiting for transfers between devices  50.1 us (10%)
  matrix products  37.5 us (7%)
    all_to_all x6, blocking collectives, own_rows(): lax.all_to_all(jnp.stack([chunk] * lax.axis_size('layer')), 'layer', 0, 0)  224 us
    concatenate x8, other arithmetic, padded(): return jnp.concatenate([before, array, after], axis=0)  55.1 us
    gather x8, local copies, waits for them, and re-layouts, own_rows(): picked = blocks[rel_own]  48.6 us
    dot_general x8, matrix products, own_rows(): jnp.einsum('rsij,rsjc->ric', h_own, picked, preferred_element_type=jnp.fl...  37.5 us
    ppermute x8, starting transfers between devices, padded(): after = lax.ppermute(array[:width], 'grid', down)  36.9 us
    all_to_all x2, waiting for transfers between devices, own_rows(): lax.all_to_all(jnp.stack([chunk] * lax.axis_size('layer')), 'layer', 0, 0)  28.2 us
    all_to_all x1, waiting for transfers between devices, shards(): h_own = lax.all_to_all(h_blocks, 'layer', 0, 1, tiled=True)  21.8 us
    slice x8, local copies, waits for them, and re-layouts, padded(): before = lax.ppermute(array[length - width:], 'grid', up)  13 us
  transfers between devices with their start and end apart: 19, of which 3 were waited for; matrix products, arithmetic and copies ran while one was open for 25% of the time, Pallas kernels for 0%

profile of v1, /device:TPU:0, one launch (start us, length us, event | category | flops | bytes accessed | tf_op | source)
XLA Modules:
  0.0 514.4 jit_solution(13680437825567032629)
XLA Ops:
  1.4 10.5 %all_to_all.77 = s32[4,8,2]{1,2,0:T(2,128)S(1)} all-to-all(s32[4,8,2]{1,2,0:T(2,128)S(1)} %copy.9), channel_id=1, replica_groups=mesh['grid'=32,'layer'=4] {'layer'}, dimensions={0} | all-to-all | bytes 512 | tf_op jit(solution)/shard_map/all_to_all | solution.py:38
  18.9 21.8 %all-to-all-done.2 = bf16[32,2,128,128]{3,2,1,0:T(8,128)(2,1)S(1)} async-done(((bf16[32,2,128,128]{3,2,1,0:T(8,128)(2,1)}), bf16[32,2,128,128]{3,2,1,0:T(8,128)(2,1)S(1)}, u32[]{:S(2)}, u32[]{:S(2)}) %all-to-all-start.2) | async-done | bytes 2097184 | tf_op jit(solution)/shard_map/all_to_all | solution.py:37
  42.6 39.0 %all_to_all.78 = bf16[4,1024,384]{2,1,0:T(8,128)(2,1)} all-to-all(bf16[4,1024,384]{2,1,0:T(8,128)(2,1)S(1)} %stack.19), channel_id=1, replica_groups=mesh['grid'=32,'layer'=4] {'layer'}, dimensions={0} | all-to-all | bytes 6291456 | tf_op jit(solution)/shard_map/all_to_all | solution.py:23
  82.0 38.0 %all_to_all.79 = bf16[4,1024,384]{2,1,0:T(8,128)(2,1)} all-to-all(bf16[4,1024,384]{2,1,0:T(8,128)(2,1)S(1)} %stack.18), channel_id=1, replica_groups=mesh['grid'=32,'layer'=4] {'layer'}, dimensions={0} | all-to-all | bytes 6291456 | tf_op jit(solution)/shard_map/all_to_all | solution.py:23
  120.3 37.0 %all_to_all.80 = bf16[4,1024,384]{2,1,0:T(8,128)(2,1)} all-to-all(bf16[4,1024,384]{2,1,0:T(8,128)(2,1)S(1)} %stack.17), channel_id=1, replica_groups=mesh['grid'=32,'layer'=4] {'layer'}, dimensions={0} | all-to-all | bytes 6291456 | tf_op jit(solution)/shard_map/all_to_all | solution.py:23
  180.8 15.7 %all-to-all-done = bf16[4,1024,384]{2,1,0:T(8,128)(2,1)} async-done(((bf16[4,1024,384]{2,1,0:T(8,128)(2,1)}), bf16[4,1024,384]{2,1,0:T(8,128)(2,1)}, u32[]{:S(2)}, u32[]{:S(2)}) %all-to-all-start) | async-done | bytes 3145760 | tf_op jit(solution)/shard_map/all_to_all | solution.py:23
  198.8 7.1 %pad_maximum_fusion.3 = bf16[4608,384]{1,0:T(8,128)(2,1)} fusion(bf16[256,384]{1,0:T(8,128)(2,1)S(1)} %collective-permute-done.7, bf16[4096,384]{1,0:T(8,128)(2,1)} %bitcast.156, bf16[256,384]{1,0:T(8,128)(2,1)S(1)} %collective-permute-done.6), kind=kLoop, calls=%fused_computation.11 | loop fusion | flops 10616832 | bytes 7077888 | tf_op jit(solution)/shard_map/concatenate | solution.py:17
  205.9 6.0 %gather_fusion.3 = bf16[64,128,384]{2,1,0:T(8,128)(2,1)} fusion(bf16[36,128,384]{2,1,0:T(8,128)(2,1)} %bitcast.140, s32[1024]{0:T(1024)S(1)} %pad_clamp_fusion), kind=kCustom, calls=%fused_computation.3 | custom fusion | bytes 12583168 | tf_op jit(solution)/shard_map/gather | solution.py:27
  216.9 7.1 %pad_maximum_fusion.2 = bf16[4608,384]{1,0:T(8,128)(2,1)} fusion(bf16[256,384]{1,0:T(8,128)(2,1)S(1)} %collective-permute-done.5, bf16[4096,384]{1,0:T(8,128)(2,1)} %bitcast.152, bf16[256,384]{1,0:T(8,128)(2,1)S(1)} %collective-permute-done.4), kind=kLoop, calls=%fused_computation.10 | loop fusion | flops 10616832 | bytes 7077888 | tf_op jit(solution)/shard_map/concatenate | solution.py:17
  224.0 6.2 %gather_fusion.2 = bf16[64,128,384]{2,1,0:T(8,128)(2,1)} fusion(bf16[36,128,384]{2,1,0:T(8,128)(2,1)} %bitcast.141, s32[1024]{0:T(1024)S(1)} %pad_clamp_fusion), kind=kCustom, calls=%fused_computation.2 | custom fusion | bytes 12583168 | tf_op jit(solution)/shard_map/gather | solution.py:27
  230.1 5.3 %bitcast_multiply_fusion.4 = f32[8,384,128]{1,2,0:T(8,128)} fusion(bf16[8,8,128,128]{3,2,1,0:T(8,128)(2,1)S(1)} %bitcast.123, bf16[8,8,128,384]{3,2,1,0:T(8,128)(2,1)} %bitcast.131), kind=kOutput, calls=%fused_computation.38 | convolution fusion | flops 805699584 | bytes 9961472 | tf_op jit(solution)/shard_map/rsij,rsjc->ric/dot_general | solution.py:28
  238.1 6.3 %pad_maximum_fusion.1 = bf16[4608,384]{1,0:T(8,128)(2,1)} fusion(bf16[256,384]{1,0:T(8,128)(2,1)S(1)} %collective-permute-done.3, bf16[4096,384]{1,0:T(8,128)(2,1)S(1)} %bitcast.148, bf16[256,384]{1,0:T(8,128)(2,1)S(1)} %collective-permute-done.2), kind=kLoop, calls=%fused_computation.9 | loop fusion | flops 10616832 | bytes 7077888 | tf_op jit(solution)/shard_map/concatenate | solution.py:17
  244.3 6.1 %gather_fusion.1 = bf16[64,128,384]{2,1,0:T(8,128)(2,1)} fusion(bf16[36,128,384]{2,1,0:T(8,128)(2,1)} %bitcast.142, s32[1024]{0:T(1024)S(1)} %pad_clamp_fusion), kind=kCustom, calls=%fused_computation.1 | custom fusion | bytes 12583168 | tf_op jit(solution)/shard_map/gather | solution.py:27
  250.5 5.2 %bitcast_multiply_fusion.6 = f32[8,384,128]{1,2,0:T(8,128)} fusion(bf16[8,8,128,128]{3,2,1,0:T(8,128)(2,1)S(1)} %bitcast.125, bf16[8,8,128,384]{3,2,1,0:T(8,128)(2,1)} %bitcast.134), kind=kOutput, calls=%fused_computation.40 | convolution fusion | flops 805699584 | bytes 9961472 | tf_op jit(solution)/shard_map/rsij,rsjc->ric/dot_general | solution.py:28
  255.7 7.3 %pad_maximum_fusion = bf16[4608,384]{1,0:T(8,128)(2,1)} fusion(bf16[256,384]{1,0:T(8,128)(2,1)S(1)} %collective-permute-done.1, bf16[4096,384]{1,0:T(8,128)(2,1)} %bitcast, bf16[256,384]{1,0:T(8,128)(2,1)S(1)} %collective-permute-done), kind=kLoop, calls=%fused_computation.8 | loop fusion | flops 10616832 | bytes 7077888 | tf_op jit(solution)/shard_map/concatenate | solution.py:17
  262.9 6.1 %gather_fusion = bf16[64,128,384]{2,1,0:T(8,128)(2,1)} fusion(bf16[36,128,384]{2,1,0:T(8,128)(2,1)} %bitcast.143, s32[1024]{0:T(1024)S(1)} %pad_clamp_fusion), kind=kCustom, calls=%fused_computation | custom fusion | bytes 12583168 | tf_op jit(solution)/shard_map/gather | solution.py:27
  275.2 37.7 %all_to_all.81 = bf16[4,1024,384]{2,1,0:T(8,128)(2,1)} all-to-all(bf16[4,1024,384]{2,1,0:T(8,128)(2,1)S(1)} %stack.23), channel_id=1, replica_groups=mesh['grid'=32,'layer'=4] {'layer'}, dimensions={0} | all-to-all | bytes 6291456 | tf_op jit(solution)/shard_map/all_to_all | solution.py:23
  313.3 36.6 %all_to_all.82 = bf16[4,1024,384]{2,1,0:T(8,128)(2,1)} all-to-all(bf16[4,1024,384]{2,1,0:T(8,128)(2,1)S(1)} %stack.22), channel_id=1, replica_groups=mesh['grid'=32,'layer'=4] {'layer'}, dimensions={0} | all-to-all | bytes 6291456 | tf_op jit(solution)/shard_map/all_to_all | solution.py:23
  350.2 35.7 %all_to_all.83 = bf16[4,1024,384]{2,1,0:T(8,128)(2,1)} all-to-all(bf16[4,1024,384]{2,1,0:T(8,128)(2,1)S(1)} %stack.21), channel_id=1, replica_groups=mesh['grid'=32,'layer'=4] {'layer'}, dimensions={0} | all-to-all | bytes 6291456 | tf_op jit(solution)/shard_map/all_to_all | solution.py:23
  396.7 6.1 %collective-permute-start.15 = (bf16[256,384]{1,0:T(8,128)(2,1)S(1)}, bf16[256,384]{1,0:T(8,128)(2,1)S(1)}, u32[]{:S(2)}, u32[]{:S(2)}) collective-permute-start(bf16[256,384]{1,0:T(8,128)(2,1)S(1)} %get-tuple-element.13), channel_id=1, source_target_pairs={{4,0},{8,4},{12,8},{16,12},{20,16},{24,20},{28,24},{32,28},{36,32}... | collective-permute-start | bytes 589832 | tf_op jit(solution)/shard_map/ppermute | solution.py:16
  411.5 12.6 %all-to-all-done.6 = bf16[4,1024,384]{2,1,0:T(8,128)(2,1)} async-done(((bf16[4,1024,384]{2,1,0:T(8,128)(2,1)}), bf16[4,1024,384]{2,1,0:T(8,128)(2,1)}, u32[]{:S(2)}, u32[]{:S(2)}) %all-to-all-start.6) | async-done | bytes 3145760 | tf_op jit(solution)/shard_map/all_to_all | solution.py:23
  425.9 8.0 %collective-permute-start.11 = (bf16[256,384]{1,0:T(8,128)(2,1)}, bf16[256,384]{1,0:T(8,128)(2,1)S(1)}, u32[]{:S(2)}, u32[]{:S(2)}) collective-permute-start(bf16[256,384]{1,0:T(8,128)(2,1)} %get-tuple-element.9), channel_id=1, source_target_pairs={{4,0},{8,4},{12,8},{16,12},{20,16},{24,20},{28,24},{32,28},{36,32}... | collective-permute-start | bytes 589832 | tf_op jit(solution)/shard_map/ppermute | solution.py:16
  433.9 7.5 %pad_maximum_fusion.7 = bf16[4608,384]{1,0:T(8,128)(2,1)} fusion(bf16[256,384]{1,0:T(8,128)(2,1)S(1)} %collective-permute-done.15, bf16[4096,384]{1,0:T(8,128)(2,1)} %bitcast.158, bf16[256,384]{1,0:T(8,128)(2,1)S(1)} %collective-permute-done.14), kind=kLoop, calls=%fused_computation.15 | loop fusion | flops 10616832 | bytes 7077888 | tf_op jit(solution)/shard_map/concatenate | solution.py:17
  441.5 6.0 %gather_fusion.7 = bf16[64,128,384]{2,1,0:T(8,128)(2,1)} fusion(bf16[36,128,384]{2,1,0:T(8,128)(2,1)} %bitcast.144, s32[1024]{0:T(1024)S(1)} %pad_clamp_fusion), kind=kCustom, calls=%fused_computation.7 | custom fusion | bytes 12583168 | tf_op jit(solution)/shard_map/gather | solution.py:27
  447.5 5.4 %bitcast_multiply_fusion = f32[8,384,128]{1,2,0:T(8,128)} fusion(bf16[8,8,128,128]{3,2,1,0:T(8,128)(2,1)S(1)} %bitcast.127, bf16[8,8,128,384]{3,2,1,0:T(8,128)(2,1)} %bitcast.136), kind=kOutput, calls=%fused_computation.34 | convolution fusion | flops 805699584 | bytes 9961472 | tf_op jit(solution)/shard_map/rsij,rsjc->ric/dot_general | solution.py:28
  458.0 6.2 %pad_maximum_fusion.6 = bf16[4608,384]{1,0:T(8,128)(2,1)} fusion(bf16[256,384]{1,0:T(8,128)(2,1)S(1)} %collective-permute-done.13, bf16[4096,384]{1,0:T(8,128)(2,1)S(1)} %bitcast.154, bf16[256,384]{1,0:T(8,128)(2,1)S(1)} %collective-permute-done.12), kind=kLoop, calls=%fused_computation.14 | loop fusion | flops 10616832 | bytes 7077888 | tf_op jit(solution)/shard_map/concatenate | solution.py:17
  464.2 6.0 %gather_fusion.6 = bf16[64,128,384]{2,1,0:T(8,128)(2,1)} fusion(bf16[36,128,384]{2,1,0:T(8,128)(2,1)} %bitcast.145, s32[1024]{0:T(1024)S(1)} %pad_clamp_fusion), kind=kCustom, calls=%fused_computation.6 | custom fusion | bytes 12583168 | tf_op jit(solution)/shard_map/gather | solution.py:27
  470.3 5.4 %bitcast_multiply_fusion.1 = f32[8,384,128]{1,2,0:T(8,128)} fusion(bf16[8,8,128,128]{3,2,1,0:T(8,128)(2,1)S(1)} %bitcast.128, bf16[8,8,128,384]{3,2,1,0:T(8,128)(2,1)} %bitcast.137), kind=kOutput, calls=%fused_computation.35 | convolution fusion | flops 805699584 | bytes 9961472 | tf_op jit(solution)/shard_map/rsij,rsjc->ric/dot_general | solution.py:28
  475.7 6.3 %pad_maximum_fusion.5 = bf16[4608,384]{1,0:T(8,128)(2,1)} fusion(bf16[256,384]{1,0:T(8,128)(2,1)S(1)} %collective-permute-done.11, bf16[4096,384]{1,0:T(8,128)(2,1)S(1)} %bitcast.150, bf16[256,384]{1,0:T(8,128)(2,1)S(1)} %collective-permute-done.10), kind=kLoop, calls=%fused_computation.13 | loop fusion | flops 10616832 | bytes 7077888 | tf_op jit(solution)/shard_map/concatenate | solution.py:17
  481.9 6.0 %gather_fusion.5 = bf16[64,128,384]{2,1,0:T(8,128)(2,1)} fusion(bf16[36,128,384]{2,1,0:T(8,128)(2,1)} %bitcast.146, s32[1024]{0:T(1024)S(1)} %pad_clamp_fusion), kind=kCustom, calls=%fused_computation.5 | custom fusion | bytes 12583168 | tf_op jit(solution)/shard_map/gather | solution.py:27
  493.1 7.3 %pad_maximum_fusion.4 = bf16[4608,384]{1,0:T(8,128)(2,1)} fusion(bf16[256,384]{1,0:T(8,128)(2,1)S(1)} %collective-permute-done.9, bf16[4096,384]{1,0:T(8,128)(2,1)} %bitcast.35, bf16[256,384]{1,0:T(8,128)(2,1)S(1)} %collective-permute-done.8), kind=kLoop, calls=%fused_computation.12 | loop fusion | flops 10616832 | bytes 7077888 | tf_op jit(solution)/shard_map/concatenate | solution.py:17
  500.5 6.1 %gather_fusion.4 = bf16[64,128,384]{2,1,0:T(8,128)(2,1)} fusion(bf16[36,128,384]{2,1,0:T(8,128)(2,1)} %bitcast.139, s32[1024]{0:T(1024)S(1)} %pad_clamp_fusion), kind=kCustom, calls=%fused_computation.4 | custom fusion | bytes 12583168 | tf_op jit(solution)/shard_map/gather | solution.py:27
  (106 shorter events, 89.4 us)
Async XLA Ops:
  11.9 28.8 %all-to-all-start.2 = ((bf16[32,2,128,128]{3,2,1,0:T(8,128)(2,1)}), bf16[32,2,128,128]{3,2,1,0:T(8,128)(2,1)S(1)}, u32[]{:S(2)}, u32[]{:S(2)}) async-start(bf16[32,2,128,128]{3,2,1,0:T(8,128)(2,1)} %param.4), calls=%async_computation.2 | async-start | bytes 4194304 | tf_op jit(solution)/shard_map/all_to_all | solution.py:37
  40.7 41.0 %copy-start.5 = (bf16[32,2,128,128]{3,2,1,0:T(8,128)(2,1)}, bf16[32,2,128,128]{3,2,1,0:T(8,128)(2,1)S(1)}, u32[]{:S(2)}) copy-start(bf16[32,2,128,128]{3,2,1,0:T(8,128)(2,1)S(1)} %all-to-all-done.2) | copy-start | bytes 6291460
  42.6 39.0 %copy-start.17 = (bf16[1024,384]{1,0:T(8,128)(2,1)S(1)}, bf16[1024,384]{1,0:T(8,128)(2,1)}, u32[]{:S(2)}) copy-start(bf16[1024,384]{1,0:T(8,128)(2,1)} %get-tuple-element.23) | copy-start | bytes 2359300
  82.0 38.0 %copy-start.16 = (bf16[1024,384]{1,0:T(8,128)(2,1)S(1)}, bf16[1024,384]{1,0:T(8,128)(2,1)}, u32[]{:S(2)}) copy-start(bf16[1024,384]{1,0:T(8,128)(2,1)} %get-tuple-element.21) | copy-start | bytes 2359300
  159.2 37.2 %all-to-all-start = ((bf16[4,1024,384]{2,1,0:T(8,128)(2,1)}), bf16[4,1024,384]{2,1,0:T(8,128)(2,1)}, u32[]{:S(2)}, u32[]{:S(2)}) async-start(bf16[4,1024,384]{2,1,0:T(8,128)(2,1)} %stack.16), calls=%async_computation | async-start | bytes 6291456 | tf_op jit(solution)/shard_map/all_to_all | solution.py:23
  167.0 31.3 %collective-permute-start.6 = (bf16[256,384]{1,0:T(8,128)(2,1)S(1)}, bf16[256,384]{1,0:T(8,128)(2,1)S(1)}, u32[]{:S(2)}, u32[]{:S(2)}) collective-permute-start(bf16[256,384]{1,0:T(8,128)(2,1)S(1)} %get-tuple-element.28), channel_id=1, source_target_pairs={{0,4},{4,8},{8,12},{12,16},{16,20},{20,24},{24,28},{28,32},{32,36}... | collective-permute-start | bytes 589832 | tf_op jit(solution)/shard_map/ppermute | solution.py:15
  167.0 31.2 %collective-permute-start.7 = (bf16[256,384]{1,0:T(8,128)(2,1)S(1)}, bf16[256,384]{1,0:T(8,128)(2,1)S(1)}, u32[]{:S(2)}, u32[]{:S(2)}) collective-permute-start(bf16[256,384]{1,0:T(8,128)(2,1)S(1)} %get-tuple-element.29), channel_id=1, source_target_pairs={{4,0},{8,4},{12,8},{16,12},{20,16},{24,20},{28,24},{32,28},{36,32}... | collective-permute-start | bytes 589832 | tf_op jit(solution)/shard_map/ppermute | solution.py:16
  173.9 38.0 %collective-permute-start.4 = (bf16[256,384]{1,0:T(8,128)(2,1)}, bf16[256,384]{1,0:T(8,128)(2,1)S(1)}, u32[]{:S(2)}, u32[]{:S(2)}) collective-permute-start(bf16[256,384]{1,0:T(8,128)(2,1)} %get-tuple-element.26), channel_id=1, source_target_pairs={{0,4},{4,8},{8,12},{12,16},{16,20},{20,24},{24,28},{28,32},{32,36}... | collective-permute-start | bytes 589832 | tf_op jit(solution)/shard_map/ppermute | solution.py:15
  173.9 43.0 %collective-permute-start.5 = (bf16[256,384]{1,0:T(8,128)(2,1)}, bf16[256,384]{1,0:T(8,128)(2,1)S(1)}, u32[]{:S(2)}, u32[]{:S(2)}) collective-permute-start(bf16[256,384]{1,0:T(8,128)(2,1)} %get-tuple-element.27), channel_id=1, source_target_pairs={{4,0},{8,4},{12,8},{16,12},{20,16},{24,20},{28,24},{32,28},{36,32}... | collective-permute-start | bytes 589832 | tf_op jit(solution)/shard_map/ppermute | solution.py:16
  180.8 57.3 %collective-permute-start.2 = (bf16[256,384]{1,0:T(8,128)(2,1)}, bf16[256,384]{1,0:T(8,128)(2,1)S(1)}, u32[]{:S(2)}, u32[]{:S(2)}) collective-permute-start(bf16[256,384]{1,0:T(8,128)(2,1)} %get-tuple-element.24), channel_id=1, source_target_pairs={{0,4},{4,8},{8,12},{12,16},{16,20},{20,24},{24,28},{28,32},{32,36}... | collective-permute-start | bytes 589832 | tf_op jit(solution)/shard_map/ppermute | solution.py:15
  198.3 39.8 %collective-permute-start.3 = (bf16[256,384]{1,0:T(8,128)(2,1)}, bf16[256,384]{1,0:T(8,128)(2,1)S(1)}, u32[]{:S(2)}, u32[]{:S(2)}) collective-permute-start(bf16[256,384]{1,0:T(8,128)(2,1)} %get-tuple-element.25), channel_id=1, source_target_pairs={{4,0},{8,4},{12,8},{16,12},{20,16},{24,20},{28,24},{32,28},{36,32}... | collective-permute-start | bytes 589832 | tf_op jit(solution)/shard_map/ppermute | solution.py:16
  198.3 57.4 %collective-permute-start = (bf16[256,384]{1,0:T(8,128)(2,1)}, bf16[256,384]{1,0:T(8,128)(2,1)S(1)}, u32[]{:S(2)}, u32[]{:S(2)}) collective-permute-start(bf16[256,384]{1,0:T(8,128)(2,1)} %get-tuple-element.18), channel_id=1, source_target_pairs={{0,4},{4,8},{8,12},{12,16},{16,20},{20,24},{24,28},{28,32},{32,36}... | collective-permute-start | bytes 589832 | tf_op jit(solution)/shard_map/ppermute | solution.py:15
  205.9 6.0 %copy-start.18 = (bf16[256,384]{1,0:T(8,128)(2,1)S(1)}, bf16[256,384]{1,0:T(8,128)(2,1)}, u32[]{:S(2)}) copy-start(bf16[256,384]{1,0:T(8,128)(2,1)} %get-tuple-element.19) | copy-start | bytes 589828
  211.9 43.7 %collective-permute-start.1 = (bf16[256,384]{1,0:T(8,128)(2,1)S(1)}, bf16[256,384]{1,0:T(8,128)(2,1)S(1)}, u32[]{:S(2)}, u32[]{:S(2)}) collective-permute-start(bf16[256,384]{1,0:T(8,128)(2,1)S(1)} %copy-done.18), channel_id=1, source_target_pairs={{4,0},{8,4},{12,8},{16,12},{20,16},{24,20},{28,24},{32,28},{36,32}... | collective-permute-start | bytes 589832 | tf_op jit(solution)/shard_map/ppermute | solution.py:16
  230.1 5.3 %copy-start = (bf16[64,128,384]{2,1,0:T(8,128)(2,1)S(1)}, bf16[64,128,384]{2,1,0:T(8,128)(2,1)}, u32[]{:S(2)}) copy-start(bf16[64,128,384]{2,1,0:T(8,128)(2,1)} %gather_fusion.2) | copy-start | bytes 18874372
  269.0 5.1 copy-start.15
  274.9 38.1 %copy-start.13 = (bf16[1024,384]{1,0:T(8,128)(2,1)}, bf16[1024,384]{1,0:T(8,128)(2,1)S(1)}, u32[]{:S(2)}) copy-start(bf16[1024,384]{1,0:T(8,128)(2,1)S(1)} %get-tuple-element.16) | copy-start | bytes 2359300
  274.9 38.1 %copy-start.14 = (bf16[1024,384]{1,0:T(8,128)(2,1)}, bf16[1024,384]{1,0:T(8,128)(2,1)S(1)}, u32[]{:S(2)}) copy-start(bf16[1024,384]{1,0:T(8,128)(2,1)S(1)} %get-tuple-element.17) | copy-start | bytes 2359300
  274.9 75.0 %copy-start.12 = (bf16[1024,384]{1,0:T(8,128)(2,1)}, bf16[1024,384]{1,0:T(8,128)(2,1)S(1)}, u32[]{:S(2)}) copy-start(bf16[1024,384]{1,0:T(8,128)(2,1)S(1)} %get-tuple-element.15) | copy-start | bytes 2359300
  387.8 36.3 %all-to-all-start.6 = ((bf16[4,1024,384]{2,1,0:T(8,128)(2,1)}), bf16[4,1024,384]{2,1,0:T(8,128)(2,1)}, u32[]{:S(2)}, u32[]{:S(2)}) async-start(bf16[4,1024,384]{2,1,0:T(8,128)(2,1)} %stack.20), calls=%async_computation.6 | async-start | bytes 6291456 | tf_op jit(solution)/shard_map/all_to_all | solution.py:23
  396.6 29.3 %collective-permute-start.14 = (bf16[256,384]{1,0:T(8,128)(2,1)S(1)}, bf16[256,384]{1,0:T(8,128)(2,1)S(1)}, u32[]{:S(2)}, u32[]{:S(2)}) collective-permute-start(bf16[256,384]{1,0:T(8,128)(2,1)S(1)} %get-tuple-element.12), channel_id=1, source_target_pairs={{0,4},{4,8},{8,12},{12,16},{16,20},{20,24},{24,28},{28,32},{32,36}... | collective-permute-start | bytes 589832 | tf_op jit(solution)/shard_map/ppermute | solution.py:15
  396.7 37.3 %collective-permute-start.15 = (bf16[256,384]{1,0:T(8,128)(2,1)S(1)}, bf16[256,384]{1,0:T(8,128)(2,1)S(1)}, u32[]{:S(2)}, u32[]{:S(2)}) collective-permute-start(bf16[256,384]{1,0:T(8,128)(2,1)S(1)} %get-tuple-element.13), channel_id=1, source_target_pairs={{4,0},{8,4},{12,8},{16,12},{20,16},{24,20},{28,24},{32,28},{36,32}... | collective-permute-start | bytes 589832 | tf_op jit(solution)/shard_map/ppermute | solution.py:16
  404.7 48.3 %collective-permute-start.12 = (bf16[256,384]{1,0:T(8,128)(2,1)}, bf16[256,384]{1,0:T(8,128)(2,1)S(1)}, u32[]{:S(2)}, u32[]{:S(2)}) collective-permute-start(bf16[256,384]{1,0:T(8,128)(2,1)} %get-tuple-element.10), channel_id=1, source_target_pairs={{0,4},{4,8},{8,12},{12,16},{16,20},{20,24},{24,28},{28,32},{32,36}... | collective-permute-start | bytes 589832 | tf_op jit(solution)/shard_map/ppermute | solution.py:15
  407.2 50.8 %collective-permute-start.13 = (bf16[256,384]{1,0:T(8,128)(2,1)}, bf16[256,384]{1,0:T(8,128)(2,1)S(1)}, u32[]{:S(2)}, u32[]{:S(2)}) collective-permute-start(bf16[256,384]{1,0:T(8,128)(2,1)} %get-tuple-element.11), channel_id=1, source_target_pairs={{4,0},{8,4},{12,8},{16,12},{20,16},{24,20},{28,24},{32,28},{36,32}... | collective-permute-start | bytes 589832 | tf_op jit(solution)/shard_map/ppermute | solution.py:16
  411.5 64.1 %collective-permute-start.10 = (bf16[256,384]{1,0:T(8,128)(2,1)}, bf16[256,384]{1,0:T(8,128)(2,1)S(1)}, u32[]{:S(2)}, u32[]{:S(2)}) collective-permute-start(bf16[256,384]{1,0:T(8,128)(2,1)} %get-tuple-element.8), channel_id=1, source_target_pairs={{0,4},{4,8},{8,12},{12,16},{16,20},{20,24},{24,28},{28,32},{32,36}... | collective-permute-start | bytes 589832 | tf_op jit(solution)/shard_map/ppermute | solution.py:15
  425.9 49.8 %collective-permute-start.11 = (bf16[256,384]{1,0:T(8,128)(2,1)}, bf16[256,384]{1,0:T(8,128)(2,1)S(1)}, u32[]{:S(2)}, u32[]{:S(2)}) collective-permute-start(bf16[256,384]{1,0:T(8,128)(2,1)} %get-tuple-element.9), channel_id=1, source_target_pairs={{4,0},{8,4},{12,8},{16,12},{20,16},{24,20},{28,24},{32,28},{36,32}... | collective-permute-start | bytes 589832 | tf_op jit(solution)/shard_map/ppermute | solution.py:16
  433.9 59.2 %collective-permute-start.8 = (bf16[256,384]{1,0:T(8,128)(2,1)}, bf16[256,384]{1,0:T(8,128)(2,1)S(1)}, u32[]{:S(2)}, u32[]{:S(2)}) collective-permute-start(bf16[256,384]{1,0:T(8,128)(2,1)} %get-tuple-element.6), channel_id=1, source_target_pairs={{0,4},{4,8},{8,12},{12,16},{16,20},{20,24},{24,28},{28,32},{32,36}... | collective-permute-start | bytes 589832 | tf_op jit(solution)/shard_map/ppermute | solution.py:15
  447.5 5.4 %copy-start.19 = (bf16[256,384]{1,0:T(8,128)(2,1)S(1)}, bf16[256,384]{1,0:T(8,128)(2,1)}, u32[]{:S(2)}) copy-start(bf16[256,384]{1,0:T(8,128)(2,1)} %get-tuple-element.7) | copy-start | bytes 589828
  447.5 10.5 %copy-start.3 = (bf16[4,1024,384]{2,1,0:T(8,128)(2,1)S(1)}, bf16[4,1024,384]{2,1,0:T(8,128)(2,1)}, u32[]{:S(2)}) copy-start(bf16[4,1024,384]{2,1,0:T(8,128)(2,1)} %all_to_all.82) | copy-start | bytes 9437188
  452.9 40.2 %collective-permute-start.9 = (bf16[256,384]{1,0:T(8,128)(2,1)S(1)}, bf16[256,384]{1,0:T(8,128)(2,1)S(1)}, u32[]{:S(2)}, u32[]{:S(2)}) collective-permute-start(bf16[256,384]{1,0:T(8,128)(2,1)S(1)} %copy-done.19), channel_id=1, source_target_pairs={{4,0},{8,4},{12,8},{16,12},{20,16},{24,20},{28,24},{32,28},{36,32}... | collective-permute-start | bytes 589832 | tf_op jit(solution)/shard_map/ppermute | solution.py:16
  470.3 5.4 %copy-start.2 = (bf16[4,1024,384]{2,1,0:T(8,128)(2,1)S(1)}, bf16[4,1024,384]{2,1,0:T(8,128)(2,1)}, u32[]{:S(2)}) copy-start(bf16[4,1024,384]{2,1,0:T(8,128)(2,1)} %all_to_all.83) | copy-start | bytes 9437188
  506.6 5.1 copy-start.10
  (7 other events, 28.3 us)
